TPU v7x, 32 devices: a whole 2x2x4 slice. The times are simulated.
32 devices in a mesh: dp: 8 (over y, x, core), tensor: 4 (over z).
Axes of the slice: x: 2, y: 2, z: 4, core: 2. Of those that a mesh axis runs over, the one named last changes fastest.
Arguments:
- inputs: bfloat16 [16384, 768], P(('dp', 'tensor')), may hold values from -6 to 6
- cotangent: bfloat16 [16384, 768], P(('dp', 'tensor')), may hold values from -6 to 6
- lengths: int32 [128], P('dp'), may hold values from 25 to 128
- block_kind: int32 [32], P('dp'), may hold values from 0 to 1
- w_qkv: bfloat16 [2, 3, 768, 768], P(None, None, None, 'tensor'), may hold values from -0.3125 to 0.3125
- qv_bias: bfloat16 [2, 2, 768], P(None, None, 'tensor'), may hold values from -3 to 3
- w_out: bfloat16 [2, 768, 768], P(None, 'tensor'), may hold values from -0.625 to 0.625
- resid_bias: bfloat16 [2, 2, 768], replicated, may hold values from -3 to 3
- norm_gain: bfloat16 [2, 2, 768], replicated, may hold values from 0.5 to 1.5
- norm_shift: bfloat16 [2, 2, 768], replicated, may hold values from -2 to 2
- w_up: bfloat16 [2, 768, 3072], P(None, None, 'tensor'), may hold values from -0.21875 to 0.21875
- up_bias: bfloat16 [2, 3072], P(None, 'tensor'), may hold values from -3 to 3
- w_down: bfloat16 [2, 3072, 768], P(None, 'tensor'), may hold values from -0.15625 to 0.15625
Outputs:
- layer_out: bfloat16 [16384, 768], P(('dp', 'tensor'))
- input_grad: float32 [16384, 768], P(('dp', 'tensor'))
- grad_w_qkv: float32 [2, 3, 768, 768], P(None, None, None, 'tensor')
- grad_qv_bias: float32 [2, 2, 768], P(None, None, 'tensor')
- grad_w_out: float32 [2, 768, 768], P(None, 'tensor')
- grad_resid_bias: float32 [2, 2, 768], replicated
- grad_norm_gain: float32 [2, 2, 768], replicated
- grad_norm_shift: float32 [2, 2, 768], replicated
- grad_w_up: float32 [2, 768, 3072], P(None, None, 'tensor')
- grad_up_bias: float32 [2, 3072], P(None, 'tensor')
- grad_w_down: float32 [2, 3072, 768], P(None, 'tensor')
Inputs may be any that keep to these rules, and one draw needn't show every extreme that they name: lengths[s] is the number of real tokens of chain s; positions from lengths[s] on are padding and are never attended to. `block_kind`: block b holds chains b * 4 to (b+1) * 4 - 1, all heavy (0) or all light (1).
All inputs are finite; a program needn't handle non-finite values.
Results may differ from a plain program's by a relative error of at most 0.019.
The roundings to bfloat16 on the way count: a program that leaves them out, or rounds other values in their place, can miss the bound.
Values may be sent and summed in bfloat16 or wider, within the bound.
No kernel may reach another device: no remote copies, remote signals or barrier semaphores. Data moves between devices by JAX's collectives and lax.ppermute only.
A program may use at most 128 MiB of HBM per device.

v0:
```python
import jax
import jax.numpy as jnp
from jax import lax
from jax.sharding import PartitionSpec as P

HEAD_DIM = 64
CHAIN = 128
BLOCK_SEQS = 4
EPSILON = 1e-05
SQRT_HALF = 0.7071067811865476
INV_ROOT_TWO_PI = 0.3989422804014327


def norm_forward(row_data, gain_rows, shift_rows):
    mean_row = jnp.mean(row_data, axis=-1, keepdims=True)
    centred = row_data - mean_row
    var_row = jnp.mean(centred * centred, axis=-1, keepdims=True)
    inv_std = lax.rsqrt(var_row + EPSILON)
    unit_rows = centred * inv_std
    return (unit_rows * gain_rows + shift_rows, unit_rows, inv_std)


def norm_backward(grad_rows, gain_rows, unit_rows, inv_std):
    scaled = grad_rows * gain_rows
    mean_first = jnp.mean(scaled, axis=-1, keepdims=True)
    mean_second = jnp.mean(scaled * unit_rows, axis=-1, keepdims=True)
    return inv_std * (scaled - mean_first - unit_rows * mean_second)


def type_sum(kind_hot, values):
    return jnp.einsum("rt,rd->td", kind_hot, values, precision=lax.Precision.HIGHEST)


def gelu_slope(values):
    return 0.5 * (1.0 + lax.erf(values * SQRT_HALF)) + values * INV_ROOT_TWO_PI * jnp.exp(
        -0.5 * values * values
    )


def split_heads(row_data, heads_here):
    return row_data.reshape(BLOCK_SEQS, CHAIN, heads_here, HEAD_DIM)


def ffn_apply(up_w, ubias_w, down_w, row_blocks, kinds):

    def step(carry, packed):
        row_data, block_type = packed
        pre_act = jnp.dot(row_data, up_w[block_type], preferred_element_type=jnp.float32) + ubias_w[
            block_type
        ].astype(jnp.float32)
        activ = jax.nn.gelu(pre_act, approximate=False).astype(jnp.bfloat16)
        return (
            carry,
            (
                pre_act,
                activ,
                jnp.dot(activ, down_w[block_type], preferred_element_type=jnp.float32),
            ),
        )

    return lax.scan(step, 0, (row_blocks, kinds))[1]


def ffn_grad(up_w, ubias_w, down_w, row_blocks, grad_blocks, pre_blocks, activ_blocks, kinds):

    def step(accums, packed):
        acc_up, acc_ubias, acc_down = accums
        row_data, grad_rows, pre_act, activ, block_type = packed
        acc_down = acc_down.at[block_type].add(
            jnp.einsum("rf,rd->fd", activ, grad_rows, preferred_element_type=jnp.float32)
        )
        d_activ = jnp.einsum(
            "rd,fd->rf", grad_rows, down_w[block_type], preferred_element_type=jnp.float32
        ).astype(jnp.bfloat16)
        d_pre = (d_activ.astype(jnp.float32) * gelu_slope(pre_act)).astype(jnp.bfloat16)
        acc_up = acc_up.at[block_type].add(
            jnp.einsum("rd,rf->df", row_data, d_pre, preferred_element_type=jnp.float32)
        )
        acc_ubias = acc_ubias.at[block_type].add(jnp.sum(d_pre.astype(jnp.float32), axis=0))
        partial_back = jnp.einsum(
            "rf,df->rd", d_pre, up_w[block_type], preferred_element_type=jnp.float32
        )
        return ((acc_up, acc_ubias, acc_down), partial_back)

    zeros_ffn = (
        jnp.zeros(up_w.shape, jnp.float32),
        jnp.zeros(ubias_w.shape, jnp.float32),
        jnp.zeros(down_w.shape, jnp.float32),
    )
    return lax.scan(step, zeros_ffn, (row_blocks, grad_blocks, pre_blocks, activ_blocks, kinds))


def local(
    inputs,
    cotangent,
    lengths,
    block_kind,
    w_qkv,
    qv_bias,
    w_out,
    resid_bias,
    norm_gain,
    norm_shift,
    w_up,
    up_bias,
    w_down,
):
    tok_dev = inputs.shape[0]
    group_rows = tok_dev * lax.axis_size("tensor")
    block_rows = BLOCK_SEQS * CHAIN
    n_blocks = group_rows // block_rows
    heads_here = w_qkv.shape[3] // HEAD_DIM
    score_scale = HEAD_DIM ** (-0.5)
    highest = lax.Precision.HIGHEST
    row_block = (lax.axis_index("tensor") * tok_dev + jnp.arange(tok_dev)) // block_rows
    block_hot = row_block[:, None] == jnp.arange(n_blocks)[None, :]
    row_kind = jnp.sum(jnp.where(block_hot, block_kind[None, :], 0), axis=1)
    kind_hot = (row_kind[:, None] == jnp.arange(2)[None, :]).astype(jnp.float32)

    def pick(kind_table):
        return jnp.dot(kind_hot, kind_table.astype(jnp.float32), precision=highest)

    key_valid = jnp.arange(CHAIN)[None, :] < lengths[:, None]
    valid_blocks = key_valid.reshape(n_blocks, BLOCK_SEQS, CHAIN)

    def scores_of(query_rows, key_rows, valid_keys):
        raw_scores = (
            jnp.einsum(
                "sqhd,skhd->shqk",
                split_heads(query_rows, heads_here),
                split_heads(key_rows, heads_here),
                preferred_element_type=jnp.float32,
            )
            * score_scale
        )
        return jnp.where(valid_keys[:, None, None, :], raw_scores, -1e30)

    gathered = lax.all_gather(inputs, "tensor", axis=0, tiled=True)
    input_blocks = gathered.reshape(n_blocks, block_rows, -1)

    def attend_forward(accums, packed):
        row_data, valid_keys, block_type = packed
        projected = jnp.einsum(
            "rd,jde->jre", row_data, w_qkv[block_type], preferred_element_type=jnp.float32
        )
        bias_pair = qv_bias[block_type].astype(jnp.float32)
        query_rows = (projected[0] + bias_pair[0]).astype(jnp.bfloat16)
        key_rows = projected[1].astype(jnp.bfloat16)
        value_rows = (projected[2] + bias_pair[1]).astype(jnp.bfloat16)
        scores = scores_of(query_rows, key_rows, valid_keys)
        row_max = jnp.max(scores, axis=-1, keepdims=True)
        log_total = row_max[..., 0] + jnp.log(jnp.sum(jnp.exp(scores - row_max), axis=-1))
        attn_probs = jnp.exp(scores - log_total[..., None]).astype(jnp.bfloat16)
        mixed = jnp.einsum(
            "shqk,skhd->sqhd",
            attn_probs,
            split_heads(value_rows, heads_here),
            preferred_element_type=jnp.float32,
        )
        mixed = mixed.reshape(block_rows, -1).astype(jnp.bfloat16)
        partial_out = jnp.dot(mixed, w_out[block_type], preferred_element_type=jnp.float32)
        return (
            accums,
            (jnp.stack([query_rows, key_rows, value_rows]), log_total, mixed, partial_out),
        )

    unused, (kept_proj, kept_total, kept_mixed, attn_parts) = lax.scan(
        attend_forward, 0, (input_blocks, valid_blocks, block_kind)
    )
    attn_rows = lax.psum_scatter(
        attn_parts.reshape(group_rows, -1), "tensor", scatter_dimension=0, tiled=True
    )
    hidden_one = inputs.astype(jnp.float32) + attn_rows + pick(resid_bias[:, 0])
    gain_one = pick(norm_gain[:, 0])
    normed, unit_one, inv_one = norm_forward(hidden_one, gain_one, pick(norm_shift[:, 0]))
    normed_low = normed.astype(jnp.bfloat16)
    gathered_norm = lax.all_gather(normed_low, "tensor", axis=0, tiled=True)
    norm_blocks = gathered_norm.reshape(n_blocks, block_rows, -1)
    kept_pre, kept_activ, ffn_parts = ffn_apply(w_up, up_bias, w_down, norm_blocks, block_kind)
    ffn_rows = lax.psum_scatter(
        ffn_parts.reshape(group_rows, -1), "tensor", scatter_dimension=0, tiled=True
    )
    hidden_two = normed + ffn_rows + pick(resid_bias[:, 1])
    gain_two = pick(norm_gain[:, 1])
    output_rows, unit_two, inv_two = norm_forward(hidden_two, gain_two, pick(norm_shift[:, 1]))
    layer_out = output_rows.astype(jnp.bfloat16)
    grad_out = cotangent.astype(jnp.float32)
    d_two = norm_backward(grad_out, gain_two, unit_two, inv_two)
    d_two_low = d_two.astype(jnp.bfloat16)
    gathered_two = lax.all_gather(d_two_low, "tensor", axis=0, tiled=True)
    two_blocks = gathered_two.reshape(n_blocks, block_rows, -1)
    (acc_up, acc_ubias, acc_down), ffn_back_parts = ffn_grad(
        w_up, up_bias, w_down, norm_blocks, two_blocks, kept_pre, kept_activ, block_kind
    )
    d_normed = (
        lax.psum_scatter(
            ffn_back_parts.reshape(group_rows, -1), "tensor", scatter_dimension=0, tiled=True
        )
        + d_two
    )
    up_total, ubias_total, down_total = (acc_up, acc_ubias, acc_down)
    d_one = norm_backward(d_normed, gain_one, unit_one, inv_one)
    gain_grads = jnp.stack(
        [type_sum(kind_hot, d_normed * unit_one), type_sum(kind_hot, grad_out * unit_two)], axis=1
    )
    shift_grads = jnp.stack([type_sum(kind_hot, d_normed), type_sum(kind_hot, grad_out)], axis=1)
    rbias_grads = jnp.stack([type_sum(kind_hot, d_one), type_sum(kind_hot, d_two)], axis=1)
    gathered_one = lax.all_gather(d_one.astype(jnp.bfloat16), "tensor", axis=0, tiled=True)
    one_blocks = gathered_one.reshape(n_blocks, block_rows, -1)

    def attend_backward(accums, packed):
        acc_qkv, acc_qv, acc_out = accums
        row_data, grad_rows, valid_keys, kept_rows, log_total, mixed, block_type = packed
        acc_out = acc_out.at[block_type].add(
            jnp.einsum("re,rd->ed", mixed, grad_rows, preferred_element_type=jnp.float32)
        )
        d_mixed = jnp.einsum(
            "rd,ed->re", grad_rows, w_out[block_type], preferred_element_type=jnp.float32
        ).astype(jnp.bfloat16)
        scores = scores_of(kept_rows[0], kept_rows[1], valid_keys)
        attn_probs = jnp.exp(scores - log_total[..., None])
        d_mixed_heads = split_heads(d_mixed, heads_here)
        d_value = jnp.einsum(
            "shqk,sqhd->skhd",
            attn_probs.astype(jnp.bfloat16),
            d_mixed_heads,
            preferred_element_type=jnp.float32,
        )
        d_value = d_value.reshape(block_rows, -1).astype(jnp.bfloat16)
        d_probs = jnp.einsum(
            "sqhd,skhd->shqk",
            d_mixed_heads,
            split_heads(kept_rows[2], heads_here),
            preferred_element_type=jnp.float32,
        )
        prob_dot = jnp.sum(attn_probs * d_probs, axis=-1, keepdims=True)
        d_scores = (attn_probs * (d_probs - prob_dot)).astype(jnp.bfloat16)
        d_query = (
            jnp.einsum(
                "shqk,skhd->sqhd",
                d_scores,
                split_heads(kept_rows[1], heads_here),
                preferred_element_type=jnp.float32,
            )
            * score_scale
        )
        d_key = (
            jnp.einsum(
                "shqk,sqhd->skhd",
                d_scores,
                split_heads(kept_rows[0], heads_here),
                preferred_element_type=jnp.float32,
            )
            * score_scale
        )
        d_query = d_query.reshape(block_rows, -1).astype(jnp.bfloat16)
        d_key = d_key.reshape(block_rows, -1).astype(jnp.bfloat16)
        d_proj = jnp.stack([d_query, d_key, d_value])
        acc_qkv = acc_qkv.at[block_type].add(
            jnp.einsum("rd,jre->jde", row_data, d_proj, preferred_element_type=jnp.float32)
        )
        bias_sums = jnp.stack(
            [
                jnp.sum(d_query.astype(jnp.float32), axis=0),
                jnp.sum(d_value.astype(jnp.float32), axis=0),
            ]
        )
        acc_qv = acc_qv.at[block_type].add(bias_sums)
        partial_back = jnp.einsum(
            "jre,jde->rd", d_proj, w_qkv[block_type], preferred_element_type=jnp.float32
        )
        return ((acc_qkv, acc_qv, acc_out), partial_back)

    zeros_attn = (
        jnp.zeros(w_qkv.shape, jnp.float32),
        jnp.zeros(qv_bias.shape, jnp.float32),
        jnp.zeros(w_out.shape, jnp.float32),
    )
    (acc_qkv, acc_qv, acc_out), qkv_back_parts = lax.scan(
        attend_backward,
        zeros_attn,
        (input_blocks, one_blocks, valid_blocks, kept_proj, kept_total, kept_mixed, block_kind),
    )
    input_grad = (
        lax.psum_scatter(
            qkv_back_parts.reshape(group_rows, -1).astype(jnp.bfloat16),
            "tensor",
            scatter_dimension=0,
            tiled=True,
        ).astype(jnp.float32)
        + d_one
    )
    qkv_total, qv_total, out_total, up_total, ubias_total, down_total = lax.psum(
        (acc_qkv, acc_qv, acc_out, up_total, ubias_total, down_total), "dp"
    )
    rbias_total, gain_total, shift_total = lax.psum(
        (rbias_grads, gain_grads, shift_grads), ("dp", "tensor")
    )
    return (
        layer_out,
        input_grad,
        qkv_total,
        qv_total,
        out_total,
        rbias_total,
        gain_total,
        shift_total,
        up_total,
        ubias_total,
        down_total,
    )


def solution(mesh):
    return jax.shard_map(
        local,
        mesh=mesh,
        in_specs=(
            P(("dp", "tensor"), None),
            P(("dp", "tensor"), None),
            P("dp"),
            P("dp"),
            P(None, None, None, "tensor"),
            P(None, None, "tensor"),
            P(None, "tensor", None),
            P(),
            P(),
            P(),
            P(None, None, "tensor"),
            P(None, "tensor"),
            P(None, "tensor", None),
        ),
        out_specs=(
            P(("dp", "tensor"), None),
            P(("dp", "tensor"), None),
            P(None, None, None, "tensor"),
            P(None, None, "tensor"),
            P(None, "tensor", None),
            P(),
            P(),
            P(),
            P(None, None, "tensor"),
            P(None, "tensor"),
            P(None, "tensor", None),
        ),
        check_vma=False,
    )
```

profile of v0, /device:TPU:0, one launch (start us, length us, event | category | flops | bytes accessed | tf_op | source)
XLA Modules:
  0.0 1168.2 jit_solution(15813986910202748736)
XLA Ops:
  8.8 67.0 %all-gather.5.cloned.1.call-done = bf16[2048,768]{1,0:T(8,128)(2,1)} async-done(((bf16[512,768]{1,0:T(8,128)(2,1)}), bf16[2048,768]{1,0:T(8,128)(2,1)}) %all-gather.5.cloned.1.call-update) | async-done | bytes 3145744 | tf_op jit(solution)/shard_map/all_gather | solution.py:138
  75.8 3.2 broadcast.348.clone
  79.0 39.6 %while.68 = (s32[]{:T(128)}, bf16[4,3,512,192]{2,3,1,0:T(8,128)(2,1)}, f32[4,4,3,128]{3,2,1,0:T(4,128)S(1)}, bf16[4,512,192]{1,2,0:T(8,128)(2,1)S(1)}, f32[4,512...) while((s32[]{:T(128)}, ...), condition=%wide.region_3.4_spmd, body=%wide.region_0.3_spmd.sunk | while | flops 658340736 | bytes 15210975 | solution.py:167
  120.6 107.5 %reduce-scatter.5.cloned.1.call-done = f32[512,768]{1,0:T(8,128)} async-done(((f32[2048,768]{1,0:T(8,128)}), f32[512,768]{1,0:T(8,128)}) %reduce-scatter.5.cloned.1.call-update) | async-done | bytes 1572880 | tf_op jit(solution)/shard_map/reduce_scatter | solution.py:170
  232.6 64.0 %all-gather.7.cloned.1.call-done = bf16[2048,768]{1,0:T(8,128)(2,1)} async-done(((bf16[512,768]{1,0:T(8,128)(2,1)}), bf16[2048,768]{1,0:T(8,128)(2,1)}) %all-gather.7.cloned.1.call-update) | async-done | bytes 3145744 | tf_op jit(solution)/shard_map/all_gather | solution.py:177
  296.6 3.2 broadcast.348.clone.1
  299.8 3.1 broadcast.348.clone.2
  303.0 48.6 %while.69 = (s32[]{:T(128)}, f32[4,512,768]{2,1,0:T(8,128)}, bf16[4,512,768]{2,1,0:T(8,128)(2,1)}, f32[4,512,768]{2,1,0:T(8,128)}, bf16[4,512,768]{2,1,0:T(8,128...) while((s32[]{:T(128)}, f32[4,512,768]{2,1,0:T(8,128)}, ...), condition=%wide.region_9.10_spmd, body=%wide.region_8.9_spmd.sunk | while | flops 1233912576 | bytes 21243096 | solution.py:61
  305.5 3.5 bitcast_dynamic-update-slice_fusion.16
  309.0 4.2 bitcast_dynamic-update-slice_fusion.17
  317.6 3.4 bitcast_dynamic-update-slice_fusion.16
  321.1 4.2 bitcast_dynamic-update-slice_fusion.17
  329.8 3.5 bitcast_dynamic-update-slice_fusion.16
  333.3 4.2 bitcast_dynamic-update-slice_fusion.17
  342.0 3.5 bitcast_dynamic-update-slice_fusion.16
  345.5 4.2 bitcast_dynamic-update-slice_fusion.17
  351.7 109.5 %reduce-scatter.7.cloned.1.call-done = f32[512,768]{1,0:T(8,128)} async-done(((f32[2048,768]{1,0:T(8,128)}), f32[512,768]{1,0:T(8,128)}) %reduce-scatter.7.cloned.1.call-update) | async-done | bytes 1572880 | tf_op jit(solution)/shard_map/reduce_scatter | solution.py:180
  467.7 63.9 %all-gather.9.cloned.1.call-done = bf16[2048,768]{1,0:T(8,128)(2,1)} async-done(((bf16[512,768]{1,0:T(8,128)(2,1)}), bf16[2048,768]{1,0:T(8,128)(2,1)}) %all-gather.9.cloned.1.call-update) | async-done | bytes 3145744 | tf_op jit(solution)/shard_map/all_gather | solution.py:190
  536.5 3.1 broadcast.348
  539.7 79.0 %while.70 = (s32[]{:T(128)}, f32[2,768,768]{2,1,0:T(8,128)}, f32[2,768]{1,0:T(2,128)S(1)}, f32[2,768,768]{2,1,0:T(8,128)}, f32[4,512,768]{2,1,0:T(8,128)}, /*ind...) while((s32[]{:T(128)}, f32[2,768,768]{2,1,0:T(8,128)}, ...), condition=%wide.region_19.20_spmd, body=%wide.region_15.19_spmd.sunk | while | flops 2423784192 | bytes 36199780 | solution.py:90
  542.2 3.1 convert_reduce_fusion.9
  546.1 4.7 fusion.226
  552.1 5.3 fusion.227
  561.9 3.1 convert_reduce_fusion.9
  565.8 4.7 fusion.226
  571.8 5.3 fusion.227
  581.7 3.1 convert_reduce_fusion.9
  585.6 4.7 fusion.226
  591.7 5.3 fusion.227
  601.4 3.1 convert_reduce_fusion.9
  605.3 4.7 fusion.226
  611.4 5.3 fusion.227
  619.2 109.0 %reduce-scatter.9.cloned.1.call-done = f32[512,768]{1,0:T(8,128)} async-done(((f32[2048,768]{1,0:T(8,128)}), f32[512,768]{1,0:T(8,128)}) %reduce-scatter.9.cloned.1.call-update) | async-done | bytes 1572880 | tf_op jit(solution)/shard_map/reduce_scatter | solution.py:196
  728.3 2.9 fusion.146
  735.0 62.2 %all-gather.11.cloned.1.call-done = bf16[2048,768]{1,0:T(8,128)(2,1)} async-done(((bf16[512,768]{1,0:T(8,128)(2,1)}), bf16[2048,768]{1,0:T(8,128)(2,1)}) %all-gather.11.cloned.1.call-update) | async-done | bytes 3145744 | tf_op jit(solution)/shard_map/all_gather | solution.py:208
  800.4 95.7 %while.71 = (s32[]{:T(128)}, f32[2,3,768,192]{2,3,1,0:T(8,128)}, f32[2,2,192]{2,1,0:T(2,128)S(1)}, f32[2,192,768]{2,1,0:T(8,128)}, bf16[4,512,768]{2,1,0:T(8,128...) while((s32[]{:T(128)}, f32[2,3,768,192]{2,3,1,0:T(8,128)}, ...), condition=%wide.region_29.30_spmd, body=%wide.region_23.29_spmd.sunk | while | flops 1337720064 | bytes 39173132 | solution.py:279
  813.6 4.2 fusion.244
  819.4 3.2 fusion.245
  837.6 4.2 fusion.244
  843.3 3.2 fusion.245
  861.5 4.2 fusion.244
  867.2 3.2 fusion.245
  885.4 4.2 fusion.244
  891.2 3.2 fusion.245
  905.5 43.0 %all-reduce = (f32[2,2,768]{2,0,1:T(2,128)S(1)}, f32[2,2,768]{2,0,1:T(2,128)S(1)}, f32[2,2,768]{2,0,1:T(2,128)S(1)}) all-reduce(f32[2,2,768]{2,0,1:T(2,128)S(1)} %pad_maximum_fusion, f32[2,2,768]{2,0,1:T(2,128)S(1)} %pad_maximum_fusion.1, f32[2,2,768]{2,0,1:T(2,128)S(1)} %pad_maximum_fusion.2), channel_id=1, replica_groups=mesh['dp'=8,'tensor'=4] {'dp','tensor'}, use_global_device_ids=true, to_apply=%region_34.35 | all-reduce | flops 9216 | bytes 73728 | tf_op jit(solution)/shard_map/psum | solution.py:296
  950.3 24.0 %all-reduce.1 = (f32[2,2,192]{2,1,0:T(2,128)}, f32[2,768]{1,0:T(2,128)}) all-reduce(f32[2,2,192]{2,1,0:T(2,128)S(1)} %get-tuple-element.342, f32[2,768]{1,0:T(2,128)S(1)} %copy-done.25), channel_id=1, replica_groups=mesh['dp'=8,'tensor'=4] {'dp'}, use_global_device_ids=true, to_apply=%region_32.33 | all-reduce | flops 2304 | bytes 18432 | tf_op jit(solution)/shard_map/psum | solution.py:293
  976.7 173.9 %all-reduce.5.cloned.1.call-done = (f32[2,3,768,192]{2,3,1,0:T(8,128)}, f32[2,192,768]{2,1,0:T(8,128)}, f32[2,768,768]{2,1,0:T(8,128)}, f32[2,768,768]{2,1,0:T(8,128)}) async-done(((f32[2,3,768,192]{2,3,1,0:T(8,128)}, f32[2,192,768]{2,1,0:T(8,128)}, f32[2,768,768]{2,1,0:T(8,128)}, f32[2,768,768]{2,1,0:T(8,128)}), (f32[2,3,768,192]{2,3,1,0:T(8,128)}, f32[2,192,768]{2,1,0:T(8,128)}, f32[2,768,768]{2,1,0:T(8,128)}, ...) | async-done | bytes 14155792 | tf_op jit(solution)/shard_map/psum | solution.py:293
  1150.6 4.3 copy.275
  (527 shorter events, 165.3 us)
Async XLA Ops:
  7.2 68.6 %all-gather.5.cloned.1.call-start = ((), (), s32[]{:S(2)}) async-start(), calls=%async_computation.4 | async-start | bytes 3932160 | tf_op jit(solution)/shard_map/all_gather | solution.py:138
  7.9 220.2 %reduce-scatter.5.cloned.1.call-start = ((), (), s32[]{:S(2)}) async-start(), calls=%async_computation.5 | async-start | bytes 7864320 | tf_op jit(solution)/shard_map/reduce_scatter | solution.py:170
  119.5 177.2 %all-gather.7.cloned.1.call-start = ((), (), s32[]{:S(2)}) async-start(), calls=%async_computation.6 | async-start | bytes 3932160 | tf_op jit(solution)/shard_map/all_gather | solution.py:177
  120.6 109.9 %copy-start.17 = (f32[512,768]{1,0:T(8,128)}, f32[512,768]{1,0:T(8,128)S(1)}, u32[]{:S(2)}) copy-start(f32[512,768]{1,0:T(8,128)S(1)} %fusion.116) | copy-start | bytes 4718596
  230.2 501.0 %copy-start = (f32[512,768]{1,0:T(8,128)}, f32[512,768]{1,0:T(8,128)S(1)}, u32[]{:S(2)}) copy-start(f32[512,768]{1,0:T(8,128)S(1)} %get-tuple-element.566) | copy-start | bytes 4718596
  230.2 501.0 %copy-start.29 = (f32[512]{0:T(512)}, f32[512]{0:T(512)S(1)}, u32[]{:S(2)}) copy-start(f32[512]{0:T(512)S(1)} %broadcast_multiply_fusion.5) | copy-start | bytes 6148
  230.6 500.7 %copy-start.33 = (f32[512]{0:T(512)}, f32[512]{0:T(512)S(1)}, u32[]{:S(2)}) copy-start(f32[512]{0:T(512)S(1)} %add_rsqrt_fusion.1) | copy-start | bytes 6148
  232.5 228.7 %reduce-scatter.7.cloned.1.call-start = ((), (), s32[]{:S(2)}) async-start(), calls=%async_computation.7 | async-start | bytes 7864320 | tf_op jit(solution)/shard_map/reduce_scatter | solution.py:180
  309.0 4.2 copy-start.51
  333.3 4.2 copy-start.51
  351.6 179.9 %all-gather.9.cloned.1.call-start = ((), (), s32[]{:S(2)}) async-start(), calls=%async_computation.8 | async-start | bytes 3932160 | tf_op jit(solution)/shard_map/all_gather | solution.py:190
  467.5 260.8 %reduce-scatter.9.cloned.1.call-start = ((), (), s32[]{:S(2)}) async-start(), calls=%async_computation.9 | async-start | bytes 7864320 | tf_op jit(solution)/shard_map/reduce_scatter | solution.py:196
  545.3 5.5 copy-start.9
  552.1 5.3 copy-start.10
  552.1 5.3 copy-start.11
  565.0 5.5 copy-start.9
  571.8 5.3 copy-start.10
  571.8 5.3 copy-start.11
  584.8 5.5 copy-start.9
  591.6 5.3 copy-start.10
  591.6 5.3 copy-start.11
  604.5 5.5 copy-start.9
  611.4 5.3 copy-start.10
  611.4 5.3 copy-start.11
  619.2 177.9 %all-gather.11.cloned.1.call-start = ((), (), s32[]{:S(2)}) async-start(), calls=%async_computation.10 | async-start | bytes 3932160 | tf_op jit(solution)/shard_map/all_gather | solution.py:208
  733.1 241.2 %reduce-scatter.11.cloned.1.call-start = ((), (), s32[]{:S(2)}) async-start(), calls=%async_computation.11 | async-start | bytes 3932160 | tf_op jit(solution)/shard_map/reduce_scatter | solution.py:285
  800.4 5.4 copy-start.49
  800.4 5.8 copy-start.35
  813.6 4.4 copy-start.39
  818.0 4.5 copy-start.20
  824.3 5.5 copy-start.49
  824.3 5.8 copy-start.35
  837.6 4.4 copy-start.39
  841.9 4.5 copy-start.20
  848.2 5.5 copy-start.49
  848.2 5.8 copy-start.35
  861.5 4.4 copy-start.39
  865.8 4.5 copy-start.20
  872.1 5.5 copy-start.49
  872.1 5.8 copy-start.35
  885.4 4.4 copy-start.39
  889.8 4.5 copy-start.20
  896.0 254.5 %all-reduce.5.cloned.1.call-start = ((), (), s32[]{:S(2)}) async-start(), calls=%async_computation.12 | async-start | bytes 28311552 | tf_op jit(solution)/shard_map/psum | solution.py:293
  904.6 45.6 %copy-start.25 = (f32[2,768]{1,0:T(2,128)S(1)}, f32[2,768]{1,0:T(2,128)}, u32[]{:S(2)}) copy-start(f32[2,768]{1,0:T(2,128)} %copy-done.24) | copy-start | bytes 18436
  904.7 69.6 %copy-start.15 = (f32[512,768]{1,0:T(8,128)S(1)}, f32[512,768]{1,0:T(8,128)}, u32[]{:S(2)}) copy-start(f32[512,768]{1,0:T(8,128)} %get-tuple-element.534) | copy-start | bytes 4718596
  1150.6 4.4 copy-start.23
  1150.6 5.4 copy-start.21
  1155.0 4.2 slice-start
  (69 other events, 144.6 us)
Sparse Core Ops, SparseCore 0:
  9.6 66.1 all-gather.4
  118.7 109.3 reduce-scatter.4
  232.6 63.9 all-gather.6
  351.7 109.4 reduce-scatter.6
  467.6 63.9 all-gather.8
  618.8 109.4 reduce-scatter.8
  733.2 63.9 all-gather.10
  896.2 59.9 reduce-scatter.10
  961.4 189.1 all-reduce.4
where the time goes:
time: 1170 us
  waiting for transfers between devices  758 us (65%)
  matrix products  172 us (15%)
  local copies, waits for them, and re-layouts  73.4 us (6%)
  blocking collectives  67 us (6%)
  other arithmetic  50 us (4%)
  loops' own time  32.5 us (3%)
  between operations  14.2 us (1%)
    psum x1, waiting for transfers between devices, local(): lax.psum((acc_qkv, acc_qv, acc_out, up_total, ubias_total, down_total), '...  174 us
    reduce_scatter x1, waiting for transfers between devices, local(): lax.psum_scatter(ffn_parts.reshape(group_rows, -1), 'tensor', scatter_dim...  110 us
    reduce_scatter x1, waiting for transfers between devices, local(): lax.psum_scatter(ffn_back_parts.reshape(group_rows, -1), 'tensor', scatte...  109 us
    reduce_scatter x1, waiting for transfers between devices, local(): lax.psum_scatter(attn_parts.reshape(group_rows, -1), 'tensor', scatter_di...  107 us
    all_gather x1, waiting for transfers between devices, local(): gathered = lax.all_gather(inputs, 'tensor', axis=0, tiled=True)  67 us
    all_gather x1, waiting for transfers between devices, local(): gathered_norm = lax.all_gather(normed_low, 'tensor', axis=0, tiled=True)  64 us
    all_gather x1, waiting for transfers between devices, local(): gathered_two = lax.all_gather(d_two_low, 'tensor', axis=0, tiled=True)  63.9 us
    all_gather x1, waiting for transfers between devices, local(): lax.all_gather(d_one.astype(jnp.bfloat16), 'tensor', axis=0, tiled=True)  62.2 us
  transfers between devices with their start and end apart: 9, of which 8 were waited for; matrix products, arithmetic and copies ran while one was open for 1% of the time, Pallas kernels for 0%

commit v1 on v0

--- a/solution.py
+++ b/solution.py
@@ -9,6 +9,12 @@
 EPSILON = 1e-05
 SQRT_HALF = 0.7071067811865476
 INV_ROOT_TWO_PI = 0.3989422804014327
+
+
+def laid_out(blocks, dim):
+    dims = list(blocks.shape[1:])
+    dims[dim] *= blocks.shape[0]
+    return jnp.moveaxis(blocks, 0, dim).reshape(dims)
 
 
 def norm_forward(row_data, gain_rows, shift_rows):
@@ -187,7 +193,19 @@
     grad_out = cotangent.astype(jnp.float32)
     d_two = norm_backward(grad_out, gain_two, unit_two, inv_two)
     d_two_low = d_two.astype(jnp.bfloat16)
-    gathered_two = lax.all_gather(d_two_low, "tensor", axis=0, tiled=True)
+    length = lax.axis_size("tensor")
+    pairs = [(i, (i + 1) % length) for i in range(length)]
+    back = [(b, a) for a, b in pairs]
+    lower, upper = ([], [])
+    for hop in range(length - 1):
+        if hop % 2 == 0:
+            lower.append(lax.ppermute(lower[-1] if lower else d_two_low, "tensor", pairs))
+        else:
+            upper.append(lax.ppermute(upper[-1] if upper else d_two_low, "tensor", back))
+    tiles = jnp.stack([*lower[::-1], d_two_low, *upper])
+    shift = lax.axis_index("tensor") - len(lower)
+    tiles = tiles[(jnp.arange(length) - shift) % length]
+    gathered_two = laid_out(tiles, 0)
     two_blocks = gathered_two.reshape(n_blocks, block_rows, -1)
     (acc_up, acc_ubias, acc_down), ffn_back_parts = ffn_grad(
         w_up, up_bias, w_down, norm_blocks, two_blocks, kept_pre, kept_activ, block_kind

time: 1170 us -> 1170 us (level)
  waiting for transfers between devices: 758 us -> 732 us
  starting transfers between devices: 0.69 us -> 18.8 us
    all_gather x1 -> x0, waiting for transfers between devices: 63.9 us -> none  [local(): gathered_two = lax.all_gather(d_two_low, 'tensor', axis=0, tiled=True)]
    ppermute x0 -> x3, waiting for transfers between devices: none -> 36.7 us  [the longest x2 35.1 us: local(): lax.ppermute(lower[-1] if lower else d_two_low, 'tensor', pairs)]
    ppermute x0 -> x3, starting transfers between devices: none -> 18.3 us  [the longest x2 16 us: local(): lax.ppermute(lower[-1] if lower else d_two_low, 'tensor', pairs)]
  transfers between devices with their start and end apart: 9 -> 11, of which waited for: 8 -> 10; matrix products, arithmetic and copies ran while one was open for 1% -> 1% of each run, Pallas kernels for 0% -> 0%
where the time goes in v1:
time: 1170 us
  waiting for transfers between devices  732 us (63%)
  matrix products  172 us (15%)
  local copies, waits for them, and re-layouts  77.7 us (7%)
  blocking collectives  67 us (6%)
  other arithmetic  53.3 us (5%)
  loops' own time  32.5 us (3%)
  starting transfers between devices  18.8 us (2%)
  between operations  14.5 us (1%)
    psum x1, waiting for transfers between devices, local(): lax.psum((acc_qkv, acc_qv, acc_out, up_total, ubias_total, down_total), '...  174 us
    reduce_scatter x1, waiting for transfers between devices, local(): lax.psum_scatter(ffn_parts.reshape(group_rows, -1), 'tensor', scatter_dim...  110 us
    reduce_scatter x1, waiting for transfers between devices, local(): lax.psum_scatter(ffn_back_parts.reshape(group_rows, -1), 'tensor', scatte...  109 us
    reduce_scatter x1, waiting for transfers between devices, local(): lax.psum_scatter(attn_parts.reshape(group_rows, -1), 'tensor', scatter_di...  107 us
    all_gather x1, waiting for transfers between devices, local(): gathered = lax.all_gather(inputs, 'tensor', axis=0, tiled=True)  67 us
    all_gather x1, waiting for transfers between devices, local(): gathered_norm = lax.all_gather(normed_low, 'tensor', axis=0, tiled=True)  64 us
    all_gather x1, waiting for transfers between devices, local(): lax.all_gather(d_one.astype(jnp.bfloat16), 'tensor', axis=0, tiled=True)  62.2 us
    psum x1, blocking collectives, local(): lax.psum((rbias_grads, gain_grads, shift_grads), ('dp', 'tensor'))  43 us
  transfers between devices with their start and end apart: 11, of which 10 were waited for; matrix products, arithmetic and copies ran while one was open for 1% of the time, Pallas kernels for 0%

profile of v1, /device:TPU:0, one launch (start us, length us, event | category | flops | bytes accessed | tf_op | source)
XLA Modules:
  0.0 1167.5 jit_solution(13195394639864961860)
XLA Ops:
  8.8 67.0 %all-gather.4.cloned.1.call-done = bf16[2048,768]{1,0:T(8,128)(2,1)} async-done(((bf16[512,768]{1,0:T(8,128)(2,1)}), bf16[2048,768]{1,0:T(8,128)(2,1)}) %all-gather.4.cloned.1.call-update) | async-done | bytes 3145744 | tf_op jit(solution)/shard_map/all_gather | solution.py:144
  75.8 3.2 broadcast.411.clone
  79.0 39.6 %while.68 = (s32[]{:T(128)}, bf16[4,3,512,192]{2,3,1,0:T(8,128)(2,1)}, f32[4,4,3,128]{3,2,1,0:T(4,128)S(1)}, bf16[4,512,192]{1,2,0:T(8,128)(2,1)S(1)}, f32[4,512...) while((s32[]{:T(128)}, ...), condition=%wide.region_3.4_spmd, body=%wide.region_0.3_spmd.sunk | while | flops 658340736 | bytes 15210975 | solution.py:173
  120.6 107.5 %reduce-scatter.5.cloned.1.call-done = f32[512,768]{1,0:T(8,128)} async-done(((f32[2048,768]{1,0:T(8,128)}), f32[512,768]{1,0:T(8,128)}) %reduce-scatter.5.cloned.1.call-update) | async-done | bytes 1572880 | tf_op jit(solution)/shard_map/reduce_scatter | solution.py:176
  232.6 64.0 %all-gather.6.cloned.1.call-done = bf16[2048,768]{1,0:T(8,128)(2,1)} async-done(((bf16[512,768]{1,0:T(8,128)(2,1)}), bf16[2048,768]{1,0:T(8,128)(2,1)}) %all-gather.6.cloned.1.call-update) | async-done | bytes 3145744 | tf_op jit(solution)/shard_map/all_gather | solution.py:183
  296.6 3.2 broadcast.411.clone.1
  299.8 3.1 broadcast.411.clone.2
  303.0 48.6 %while.69 = (s32[]{:T(128)}, f32[4,512,768]{2,1,0:T(8,128)}, bf16[4,512,768]{2,1,0:T(8,128)(2,1)}, f32[4,512,768]{2,1,0:T(8,128)}, bf16[4,512,768]{2,1,0:T(8,128...) while((s32[]{:T(128)}, f32[4,512,768]{2,1,0:T(8,128)}, ...), condition=%wide.region_9.10_spmd, body=%wide.region_8.9_spmd.sunk | while | flops 1233912576 | bytes 21243096 | solution.py:67
  305.5 3.5 bitcast_dynamic-update-slice_fusion.16
  309.0 4.2 bitcast_dynamic-update-slice_fusion.17
  317.6 3.4 bitcast_dynamic-update-slice_fusion.16
  321.1 4.2 bitcast_dynamic-update-slice_fusion.17
  329.8 3.5 bitcast_dynamic-update-slice_fusion.16
  333.3 4.2 bitcast_dynamic-update-slice_fusion.17
  342.0 3.5 bitcast_dynamic-update-slice_fusion.16
  345.5 4.2 bitcast_dynamic-update-slice_fusion.17
  351.7 109.5 %reduce-scatter.7.cloned.1.call-done = f32[512,768]{1,0:T(8,128)} async-done(((f32[2048,768]{1,0:T(8,128)}), f32[512,768]{1,0:T(8,128)}) %reduce-scatter.7.cloned.1.call-update) | async-done | bytes 1572880 | tf_op jit(solution)/shard_map/reduce_scatter | solution.py:186
  471.3 18.7 %collective-permute-done = bf16[512,768]{1,0:T(8,128)(2,1)} collective-permute-done((bf16[512,768]{1,0:T(8,128)(2,1)}, bf16[512,768]{1,0:T(8,128)(2,1)}, u32[]{:S(2)}, u32[]{:S(2)}) %collective-permute-start) | collective-permute-done | bytes 786464 | tf_op jit(solution)/shard_map/ppermute | solution.py:202
  490.0 14.5 %collective-permute-start.1 = (bf16[512,768]{1,0:T(8,128)(2,1)}, bf16[512,768]{1,0:T(8,128)(2,1)}, u32[]{:S(2)}, u32[]{:S(2)}) collective-permute-start(bf16[512,768]{1,0:T(8,128)(2,1)} %collective-permute-done), channel_id=1, source_target_pairs={{0,1},{1,2},{2,3},{3,0},{4,5},{5,6},{6,7},{7,4},{8,9},{9,10},{10,1... | collective-permute-start | bytes 2359304 | tf_op jit(solution)/shard_map/ppermute | solution.py:202
  506.2 16.3 %collective-permute-done.1 = bf16[512,768]{1,0:T(8,128)(2,1)} collective-permute-done((bf16[512,768]{1,0:T(8,128)(2,1)}, bf16[512,768]{1,0:T(8,128)(2,1)}, u32[]{:S(2)}, u32[]{:S(2)}) %collective-permute-start.1) | collective-permute-done | bytes 786464 | tf_op jit(solution)/shard_map/ppermute | solution.py:202
  522.5 3.2 pad_maximum_fusion
  525.7 4.4 gather_fusion
  535.1 3.1 broadcast.411
  538.2 79.0 %while.70 = (s32[]{:T(128)}, f32[2,768,768]{2,1,0:T(8,128)}, f32[2,768]{1,0:T(2,128)S(1)}, f32[2,768,768]{2,1,0:T(8,128)}, f32[4,512,768]{2,1,0:T(8,128)}, /*ind...) while((s32[]{:T(128)}, f32[2,768,768]{2,1,0:T(8,128)}, ...), condition=%wide.region_19.20_spmd, body=%wide.region_15.19_spmd.sunk | while | flops 2423784192 | bytes 36199780 | solution.py:96
  544.6 4.7 fusion.228
  550.7 5.3 fusion.229
  560.4 3.1 convert_reduce_fusion.9
  564.3 4.7 fusion.228
  570.4 5.3 fusion.229
  584.1 4.7 fusion.228
  590.2 5.3 fusion.229
  603.9 4.7 fusion.228
  609.9 5.3 fusion.229
  617.8 109.5 %reduce-scatter.9.cloned.1.call-done = f32[512,768]{1,0:T(8,128)} async-done(((f32[2048,768]{1,0:T(8,128)}), f32[512,768]{1,0:T(8,128)}) %reduce-scatter.9.cloned.1.call-update) | async-done | bytes 1572880 | tf_op jit(solution)/shard_map/reduce_scatter | solution.py:214
  734.0 62.2 %all-gather.8.cloned.1.call-done = bf16[2048,768]{1,0:T(8,128)(2,1)} async-done(((bf16[512,768]{1,0:T(8,128)(2,1)}), bf16[2048,768]{1,0:T(8,128)(2,1)}) %all-gather.8.cloned.1.call-update) | async-done | bytes 3145744 | tf_op jit(solution)/shard_map/all_gather | solution.py:226
  799.4 95.7 %while.71 = (s32[]{:T(128)}, f32[2,3,768,192]{2,3,1,0:T(8,128)}, f32[2,2,192]{2,1,0:T(2,128)S(1)}, f32[2,192,768]{2,1,0:T(8,128)}, bf16[4,512,768]{2,1,0:T(8,128...) while((s32[]{:T(128)}, f32[2,3,768,192]{2,3,1,0:T(8,128)}, ...), condition=%wide.region_29.30_spmd, body=%wide.region_23.29_spmd.sunk | while | flops 1337720064 | bytes 39173132 | solution.py:297
  812.7 4.2 fusion.246
  818.4 3.2 fusion.247
  836.6 4.2 fusion.246
  842.3 3.2 fusion.247
  860.5 4.2 fusion.246
  866.2 3.2 fusion.247
  884.4 4.2 fusion.246
  890.2 3.2 fusion.247
  904.5 43.0 %all-reduce = (f32[2,2,768]{2,0,1:T(2,128)S(1)}, f32[2,2,768]{2,0,1:T(2,128)S(1)}, f32[2,2,768]{2,0,1:T(2,128)S(1)}) all-reduce(f32[2,2,768]{2,0,1:T(2,128)S(1)} %pad_maximum_fusion.1, f32[2,2,768]{2,0,1:T(2,128)S(1)} %pad_maximum_fusion.2, f32[2,2,768]{2,0,1:T(2,128)S(1)} %pad_maximum_fusion.3), channel_id=1, replica_groups=mesh['dp'=8,'tensor'=4] {'dp','tensor'}, use_global_device_ids=true, to_apply=%region_34.35 | all-reduce | flops 9216 | bytes 73728 | tf_op jit(solution)/shard_map/psum | solution.py:314
  949.3 24.0 %all-reduce.1 = (f32[2,2,192]{2,1,0:T(2,128)}, f32[2,768]{1,0:T(2,128)}) all-reduce(f32[2,2,192]{2,1,0:T(2,128)S(1)} %get-tuple-element.342, f32[2,768]{1,0:T(2,128)S(1)} %copy-done.25), channel_id=1, replica_groups=mesh['dp'=8,'tensor'=4] {'dp'}, use_global_device_ids=true, to_apply=%region_32.33 | all-reduce | flops 2304 | bytes 18432 | tf_op jit(solution)/shard_map/psum | solution.py:311
  975.8 173.8 %all-reduce.5.cloned.1.call-done = (f32[2,3,768,192]{2,3,1,0:T(8,128)}, f32[2,192,768]{2,1,0:T(8,128)}, f32[2,768,768]{2,1,0:T(8,128)}, f32[2,768,768]{2,1,0:T(8,128)}) async-done(((f32[2,3,768,192]{2,3,1,0:T(8,128)}, f32[2,192,768]{2,1,0:T(8,128)}, f32[2,768,768]{2,1,0:T(8,128)}, f32[2,768,768]{2,1,0:T(8,128)}), (f32[2,3,768,192]{2,3,1,0:T(8,128)}, f32[2,192,768]{2,1,0:T(8,128)}, f32[2,768,768]{2,1,0:T(8,128)}, ...) | async-done | bytes 14155792 | tf_op jit(solution)/shard_map/psum | solution.py:311
  1149.6 4.3 copy.275
  (534 shorter events, 182.8 us)
Async XLA Ops:
  7.2 68.6 %all-gather.4.cloned.1.call-start = ((), (), s32[]{:S(2)}) async-start(), calls=%async_computation.4 | async-start | bytes 3932160 | tf_op jit(solution)/shard_map/all_gather | solution.py:144
  7.9 220.2 %reduce-scatter.5.cloned.1.call-start = ((), (), s32[]{:S(2)}) async-start(), calls=%async_computation.5 | async-start | bytes 7864320 | tf_op jit(solution)/shard_map/reduce_scatter | solution.py:176
  119.5 177.2 %all-gather.6.cloned.1.call-start = ((), (), s32[]{:S(2)}) async-start(), calls=%async_computation.6 | async-start | bytes 3932160 | tf_op jit(solution)/shard_map/all_gather | solution.py:183
  120.6 109.9 %copy-start.17 = (f32[512,768]{1,0:T(8,128)}, f32[512,768]{1,0:T(8,128)S(1)}, u32[]{:S(2)}) copy-start(f32[512,768]{1,0:T(8,128)S(1)} %fusion.116) | copy-start | bytes 4718596
  230.2 500.0 %copy-start = (f32[512,768]{1,0:T(8,128)}, f32[512,768]{1,0:T(8,128)S(1)}, u32[]{:S(2)}) copy-start(f32[512,768]{1,0:T(8,128)S(1)} %get-tuple-element.566) | copy-start | bytes 4718596
  230.2 500.0 %copy-start.29 = (f32[512]{0:T(512)}, f32[512]{0:T(512)S(1)}, u32[]{:S(2)}) copy-start(f32[512]{0:T(512)S(1)} %broadcast_multiply_fusion.5) | copy-start | bytes 6148
  230.6 499.7 %copy-start.33 = (f32[512]{0:T(512)}, f32[512]{0:T(512)S(1)}, u32[]{:S(2)}) copy-start(f32[512]{0:T(512)S(1)} %add_rsqrt_fusion.1) | copy-start | bytes 6148
  232.5 228.7 %reduce-scatter.7.cloned.1.call-start = ((), (), s32[]{:S(2)}) async-start(), calls=%async_computation.7 | async-start | bytes 7864320 | tf_op jit(solution)/shard_map/reduce_scatter | solution.py:186
  351.6 375.7 %reduce-scatter.9.cloned.1.call-start = ((), (), s32[]{:S(2)}) async-start(), calls=%async_computation.8 | async-start | bytes 7864320 | tf_op jit(solution)/shard_map/reduce_scatter | solution.py:214
  467.4 22.6 %collective-permute-start = (bf16[512,768]{1,0:T(8,128)(2,1)}, bf16[512,768]{1,0:T(8,128)(2,1)}, u32[]{:S(2)}, u32[]{:S(2)}) collective-permute-start(bf16[512,768]{1,0:T(8,128)(2,1)} %get-tuple-element.536), channel_id=1, source_target_pairs={{0,1},{1,2},{2,3},{3,0},{4,5},{5,6},{6,7},{7,4},{8,9},{9,10},{10,1... | collective-permute-start | bytes 2359304 | tf_op jit(solution)/shard_map/ppermute | solution.py:202
  468.9 37.3 %collective-permute-start.2 = (bf16[512,768]{1,0:T(8,128)(2,1)}, bf16[512,768]{1,0:T(8,128)(2,1)}, u32[]{:S(2)}, u32[]{:S(2)}) collective-permute-start(bf16[512,768]{1,0:T(8,128)(2,1)} %get-tuple-element.536), channel_id=1, source_target_pairs={{1,0},{2,1},{3,2},{0,3},{5,4},{6,5},{7,6},{4,7},{9,8},{10,9},{11,1... | collective-permute-start | bytes 2359304 | tf_op jit(solution)/shard_map/ppermute | solution.py:204
  490.0 32.5 %collective-permute-start.1 = (bf16[512,768]{1,0:T(8,128)(2,1)}, bf16[512,768]{1,0:T(8,128)(2,1)}, u32[]{:S(2)}, u32[]{:S(2)}) collective-permute-start(bf16[512,768]{1,0:T(8,128)(2,1)} %collective-permute-done), channel_id=1, source_target_pairs={{0,1},{1,2},{2,3},{3,0},{4,5},{5,6},{6,7},{7,4},{8,9},{9,10},{10,1... | collective-permute-start | bytes 2359304 | tf_op jit(solution)/shard_map/ppermute | solution.py:202
  543.8 5.5 copy-start.9
  550.6 5.3 copy-start.10
  550.6 5.3 copy-start.11
  563.5 5.5 copy-start.9
  570.3 5.3 copy-start.10
  570.4 5.3 copy-start.11
  583.4 5.5 copy-start.9
  590.2 5.3 copy-start.10
  590.2 5.3 copy-start.11
  603.1 5.5 copy-start.9
  609.9 5.3 copy-start.10
  609.9 5.3 copy-start.11
  617.8 178.4 %all-gather.8.cloned.1.call-start = ((), (), s32[]{:S(2)}) async-start(), calls=%async_computation.9 | async-start | bytes 3932160 | tf_op jit(solution)/shard_map/all_gather | solution.py:226
  732.1 241.2 %reduce-scatter.11.cloned.1.call-start = ((), (), s32[]{:S(2)}) async-start(), calls=%async_computation.10 | async-start | bytes 3932160 | tf_op jit(solution)/shard_map/reduce_scatter | solution.py:303
  799.4 5.4 copy-start.49
  799.4 5.8 copy-start.35
  812.7 4.4 copy-start.39
  817.0 4.5 copy-start.20
  823.3 5.5 copy-start.49
  823.3 5.8 copy-start.35
  836.6 4.4 copy-start.39
  841.0 4.5 copy-start.20
  847.2 5.5 copy-start.49
  847.2 5.8 copy-start.35
  860.5 4.4 copy-start.39
  864.9 4.5 copy-start.20
  871.1 5.5 copy-start.49
  871.2 5.8 copy-start.35
  884.4 4.4 copy-start.39
  888.8 4.5 copy-start.20
  895.1 254.5 %all-reduce.5.cloned.1.call-start = ((), (), s32[]{:S(2)}) async-start(), calls=%async_computation.11 | async-start | bytes 28311552 | tf_op jit(solution)/shard_map/psum | solution.py:311
  903.7 45.7 %copy-start.25 = (f32[2,768]{1,0:T(2,128)S(1)}, f32[2,768]{1,0:T(2,128)}, u32[]{:S(2)}) copy-start(f32[2,768]{1,0:T(2,128)} %copy-done.24) | copy-start | bytes 18436
  903.7 69.7 %copy-start.15 = (f32[512,768]{1,0:T(8,128)S(1)}, f32[512,768]{1,0:T(8,128)}, u32[]{:S(2)}) copy-start(f32[512,768]{1,0:T(8,128)} %get-tuple-element.534) | copy-start | bytes 4718596
  1149.6 4.4 copy-start.23
  1149.6 5.4 copy-start.21
  1154.0 4.2 slice-start
  (71 other events, 152.9 us)
Sparse Core Ops, SparseCore 0:
  9.6 66.1 all-gather.3
  118.7 109.3 reduce-scatter.4
  232.6 63.9 all-gather.5
  351.7 109.4 reduce-scatter.6
  617.3 109.8 reduce-scatter.8
  732.2 63.9 all-gather.7
  895.2 59.9 reduce-scatter.10
  960.4 189.1 all-reduce.4
